TPU v7x, 512 devices: a whole 4x8x8 slice. The times are simulated.
512 devices in a mesh: grp: 4 (over x), dev: 128 (over y, z, core).
Axes of the slice: x: 4, y: 8, z: 8, core: 2. Of those that a mesh axis runs over, the one named last changes fastest.
Arguments:
- queries: bfloat16 [131072, 768], P(('grp', 'dev')), parts along dimension 0, may hold values from -10 to 10
- keys: bfloat16 [131072, 384], P(('grp', 'dev')), parts along dimension 0, may hold values from -10 to 10
- values: bfloat16 [131072, 384], P(('grp', 'dev')), parts along dimension 0, may hold values from -6 to 6
- deal_index: int32 [131072], P(('grp', 'dev')), parts along dimension 0, may hold values from 0 to 32767, as said below
- segments: int32 [512, 256], P(('grp', 'dev')), parts along dimension 0, may hold values from 0 to 3, as said below
- page_owner: int32 [512, 128], P(('grp', 'dev')), parts along dimension 0, may hold values from 0 to 127, as said below
Outputs:
- attended: bfloat16 [131072, 768], P(('grp', 'dev')), parts along dimension 0
- cache: bfloat16 [131072, 768], P(('grp', 'dev')), parts along dimension 0
There are 4 independent parts, one for each index of `grp`. A program takes and returns all parts, laid end to end along the dimension named above; each array names one. Nothing has to cross between parts.
Inputs may be any that keep to these rules, and one draw needn't show every extreme that they name: Each dealt row once; a token at row i of its arrival device has deal_index // 256 = i // 2. `segments`: along a device's rows the numbers never fall, each of 0 to 3 appears, and each request holds 32 rows or more. `page_owner`: every row and every column names each device once.
All inputs are finite; a program needn't handle non-finite values.
Results may differ from a plain program's by a relative error of at most 0.0061.
Values may be sent and summed in bfloat16 or wider, within the bound.
No kernel may reach another device: no remote copies, remote signals or barrier semaphores. Data moves between devices by JAX's collectives and lax.ppermute only.
A program may use at most 64 MiB of HBM per device.

v0:
```python
import math

import jax
import jax.numpy as jnp
from jax import lax
from jax.sharding import PartitionSpec as P

QUERY_HEAD_COUNT = 8
KEY_VALUE_HEADS = 4


ROPE_BASE = 100000.0
NEG_FILL = -1e30


def positions_of(request_labels):
    row_width = request_labels.shape[0]
    counter = jnp.arange(row_width, dtype=jnp.int32)
    boundary = jnp.concatenate(
        [jnp.ones((1,), jnp.bool_), request_labels[1:] != request_labels[:-1]]
    )
    starts = lax.cummax(jnp.where(boundary, counter, jnp.zeros_like(counter)), axis=0)
    return counter - starts


def apply_rotary(features, token_positions, head_count):
    head_depth = features.shape[1] // head_count
    half_depth = head_depth // 2
    freqs = ROPE_BASE ** (-2.0 * jnp.arange(half_depth, dtype=jnp.float32) / head_depth)
    angles = token_positions.astype(jnp.float32)[:, None] * freqs[None, :]
    cosine = jnp.cos(angles)[:, None, :]
    sine = jnp.sin(angles)[:, None, :]
    split_heads = features.astype(jnp.float32).reshape(features.shape[0], head_count, head_depth)
    first = split_heads[..., :half_depth]
    second = split_heads[..., half_depth:]
    turned = jnp.concatenate(
        [first * cosine - second * sine, second * cosine + first * sine], axis=-1
    )
    return turned.reshape(features.shape).astype(jnp.bfloat16)


def attend_heads(query_turned, query_rows, key_turned, value_matrix, request_labels, kv_heads):
    row_total = query_turned.shape[0]
    key_total = key_turned.shape[0]
    head_depth = key_turned.shape[1] // kv_heads
    group_size = query_turned.shape[1] // (kv_heads * head_depth)
    query_heads = query_turned.reshape(row_total, kv_heads, group_size, head_depth).transpose(
        1, 0, 2, 3
    )
    key_heads = key_turned.reshape(key_total, kv_heads, head_depth).transpose(1, 0, 2)
    value_heads = value_matrix.reshape(key_total, kv_heads, head_depth).transpose(1, 0, 2)
    key_index = jnp.arange(key_total, dtype=jnp.int32)
    allowed = (request_labels[query_rows][:, None] == request_labels[None, :]) & (
        key_index[None, :] <= query_rows[:, None]
    )
    logit_scale = 1.0 / math.sqrt(head_depth)

    def one_head(operands):
        query_slice, key_slice, value_slice = operands
        attention_logits = (
            jnp.einsum("qhs,bs->hqb", query_slice, key_slice, preferred_element_type=jnp.float32)
            * logit_scale
        )
        attention_logits = jnp.where(allowed[None], attention_logits, NEG_FILL)
        highest = jnp.max(attention_logits, axis=-1, keepdims=True)
        expo = jnp.exp(attention_logits - highest)
        attention_weights = (expo / jnp.sum(expo, axis=-1, keepdims=True)).astype(jnp.bfloat16)
        return jnp.einsum(
            "vjn,ne->jve", attention_weights, value_slice, preferred_element_type=jnp.float32
        )

    output_rows = lax.map(one_head, (query_heads, key_heads, value_heads))
    return output_rows.transpose(1, 0, 2, 3).reshape(row_total, -1).astype(jnp.bfloat16)


def per_device(queries, keys, values, deal_index, segments, page_owner):
    device_count = lax.axis_size("dev")
    my_index = lax.axis_index("dev")
    row_count = queries.shape[0]
    page_rows = row_count // device_count
    query_width = queries.shape[1]
    key_width = keys.shape[1]
    request_labels = segments[0]
    token_positions = positions_of(request_labels)
    gathered_rows = jnp.arange(row_count, dtype=jnp.int32)
    grouped_index = deal_index.reshape(device_count, page_rows)
    owner_row = page_owner[0]
    owner_column = owner_row.reshape(device_count, 1)

    def place(received, local_rows):
        flat_rows = received.reshape(row_count, received.shape[-1])
        return (
            jnp.zeros((row_count, received.shape[-1]), received.dtype).at[local_rows].set(flat_rows)
        )

    arrived_queries, arrived_keys, arrived_values, arrived_index, arrived_owner = (
        lax.all_to_all(
            queries.reshape(device_count, page_rows, query_width),
            "dev",
            split_axis=0,
            concat_axis=0,
            tiled=True,
        ),
        lax.all_to_all(
            keys.reshape(device_count, page_rows, key_width),
            "dev",
            split_axis=0,
            concat_axis=0,
            tiled=True,
        ),
        lax.all_to_all(
            values.reshape(device_count, page_rows, key_width),
            "dev",
            split_axis=0,
            concat_axis=0,
            tiled=True,
        ),
        lax.all_to_all(grouped_index, "dev", split_axis=0, concat_axis=0, tiled=True),
        lax.all_to_all(owner_column, "dev", split_axis=0, concat_axis=0, tiled=True),
    )
    local_rows = arrived_index.reshape(-1) - my_index * row_count
    dealt_queries = place(arrived_queries, local_rows)
    shuffled_keys = place(arrived_keys, local_rows)
    shuffled_values = place(arrived_values, local_rows)
    key_turned = apply_rotary(shuffled_keys, token_positions, KEY_VALUE_HEADS)
    query_turned = apply_rotary(dealt_queries, token_positions, QUERY_HEAD_COUNT)
    output_rows = attend_heads(
        query_turned, gathered_rows, key_turned, shuffled_values, request_labels, KEY_VALUE_HEADS
    )
    going_back = output_rows[local_rows].reshape(device_count, page_rows, query_width)
    attended = lax.all_to_all(going_back, "dev", split_axis=0, concat_axis=0, tiled=True).reshape(
        row_count, query_width
    )
    stored = jnp.concatenate([key_turned, shuffled_values], axis=1)[local_rows].reshape(
        device_count, page_rows, 2 * key_width
    )
    owner_order = jnp.argsort(arrived_owner.reshape(-1))
    sent_pages, labels = (
        lax.all_to_all(stored[owner_order], "dev", split_axis=0, concat_axis=0, tiled=True),
        lax.all_to_all(
            owner_order.reshape(device_count, 1), "dev", split_axis=0, concat_axis=0, tiled=True
        ),
    )
    placed = (
        jnp.zeros((device_count, page_rows, 2 * key_width), sent_pages.dtype)
        .at[labels.reshape(-1)]
        .set(sent_pages)
    )
    cache = placed.reshape(row_count, 2 * key_width)
    return (attended, cache)


def solution(mesh):
    in_specs = (
        P(("grp", "dev"), None),
        P(("grp", "dev"), None),
        P(("grp", "dev"), None),
        P(("grp", "dev")),
        P(("grp", "dev"), None),
        P(("grp", "dev"), None),
    )
    out_specs = (P(("grp", "dev"), None), P(("grp", "dev"), None))
    return jax.shard_map(
        per_device, mesh=mesh, in_specs=in_specs, out_specs=out_specs, check_vma=False
    )
```

profile of v0, /device:TPU:6, one launch (start us, length us, event | category | flops | bytes accessed | tf_op | source)
XLA Modules:
  0.0 182.3 jit_solution(4013974274649894157)
XLA Ops:
  0.6 0.6 copy-done.5
  1.3 0.7 copy.44
  2.0 17.9 %all-to-all-start.5 = ((s32[128,1,1]{2,1,0:T(1,128)}), s32[128,1,1]{2,1,0:T(1,128)S(1)}, u32[]{:S(2)}, u32[]{:S(2)}) async-start(s32[128,1,1]{2,1,0:T(1,128)} %copy.44), calls=%async_computation.5 | async-start | bytes 131072 | tf_op jit(solution)/shard_map/all_to_all | solution.py:119
  20.2 0.3 reduce-window.9
  20.6 0.1 slice_reduce_fusion
  20.7 0.8 all_to_all.35
  21.5 9.7 %all-to-all-done.5 = s32[128,1,1]{2,1,0:T(1,128)S(1)} async-done(((s32[128,1,1]{2,1,0:T(1,128)}), s32[128,1,1]{2,1,0:T(1,128)S(1)}, u32[]{:S(2)}, u32[]{:S(2)}) %all-to-all-start.5) | async-done | bytes 544 | tf_op jit(solution)/shard_map/all_to_all | solution.py:119
  31.1 6.1 %all-to-all-start = ((s32[128,1,2]{2,1,0:T(1,128)}), s32[128,1,2]{2,1,0:T(1,128)S(1)}, u32[]{:S(2)}, u32[]{:S(2)}) async-start(s32[128,1,2]{2,1,0:T(1,128)} %bitcast), calls=%async_computation | async-start | bytes 131072 | tf_op jit(solution)/shard_map/all_to_all | solution.py:118
  37.4 0.7 reshape.215
  38.1 10.4 %all-to-all-done = s32[128,1,2]{2,1,0:T(1,128)S(1)} async-done(((s32[128,1,2]{2,1,0:T(1,128)}), s32[128,1,2]{2,1,0:T(1,128)S(1)}, u32[]{:S(2)}, u32[]{:S(2)}) %all-to-all-start) | async-done | bytes 1056 | tf_op jit(solution)/shard_map/all_to_all | solution.py:118
  48.5 6.2 %all-to-all-start.2 = ((bf16[128,2,384]{2,1,0:T(2,128)(2,1)}), bf16[128,2,384]{2,1,0:T(2,128)(2,1)S(1)}, u32[]{:S(2)}, u32[]{:S(2)}) async-start(bf16[128,2,384]{2,1,0:T(2,128)(2,1)} %reshape.215), calls=%async_computation.2 | async-start | bytes 393216 | tf_op jit(solution)/shard_map/all_to_all | solution.py:104
  54.7 0.9 reshape.220
  55.6 0.8 reshape.212
  56.4 1.9 %gather_fusion = s32[256]{0:T(256)S(1)} fusion(s32[256]{0:T(256)S(1)} %bitcast.84, s32[1024]{0:T(1024)S(1)} %pad_clamp_fusion.2), kind=kCustom, calls=%fused_computation | custom fusion | bytes 3072 | tf_op jit(solution)/shard_map/gather | solution.py:53
  58.3 0.3 multiply_cosine_fusion
  58.6 2.4 %reduce.3 = s32[128]{0:T(128)S(1)} reduce(s32[128,1,1]{2,1,0:T(1,128)S(1)} %all-to-all-done.5, s32[]{:T(128)} %constant.11.clone.1), dimensions={1,2}, to_apply=%all_to_all.42.reduce_sub_computation | reduce | bytes 1028 | tf_op jit(solution)/shard_map/all_to_all | solution.py:119
  61.0 2.6 %sort.17 = (s32[128]{0:T(128)}, s32[128]{0:T(128)S(1)}) sort(s32[128]{0:T(128)S(1)} %reduce.3, s32[128]{0:T(128)S(1)} %iota.47), dimensions={0}, to_apply=%region_9.10 | sort | flops 896 | bytes 2048 | tf_op jit(solution)/shard_map/jit(argsort)/sort | solution.py:137
  63.6 0.7 copy.45
  64.3 4.1 %all-to-all-done.2 = bf16[128,2,384]{2,1,0:T(2,128)(2,1)S(1)} async-done(((bf16[128,2,384]{2,1,0:T(2,128)(2,1)}), bf16[128,2,384]{2,1,0:T(2,128)(2,1)S(1)}, u32[]{:S(2)}, u32[]{:S(2)}) %all-to-all-start.2) | async-done | bytes 196640 | tf_op jit(solution)/shard_map/all_to_all | solution.py:104
  68.4 9.7 %all-to-all-start.1 = ((bf16[128,2,384]{2,1,0:T(2,128)(2,1)}), bf16[128,2,384]{2,1,0:T(2,128)(2,1)S(1)}, u32[]{:S(2)}, u32[]{:S(2)}) async-start(bf16[128,2,384]{2,1,0:T(2,128)(2,1)} %reshape.212), calls=%async_computation.1 | async-start | bytes 393216 | tf_op jit(solution)/shard_map/all_to_all | solution.py:111
  78.1 0.2 subtract_reduce_fusion
  78.3 0.1 sub.39
  78.4 13.4 %all-to-all-done.1 = bf16[128,2,384]{2,1,0:T(2,128)(2,1)S(1)} async-done(((bf16[128,2,384]{2,1,0:T(2,128)(2,1)}), bf16[128,2,384]{2,1,0:T(2,128)(2,1)S(1)}, u32[]{:S(2)}, u32[]{:S(2)}) %all-to-all-start.1) | async-done | bytes 196640 | tf_op jit(solution)/shard_map/all_to_all | solution.py:111
  91.7 6.4 %all-to-all-start.3 = ((bf16[128,2,768]{2,1,0:T(2,128)(2,1)}), bf16[128,2,768]{2,1,0:T(2,128)(2,1)S(1)}, u32[]{:S(2)}, u32[]{:S(2)}) async-start(bf16[128,2,768]{2,1,0:T(2,128)(2,1)} %reshape.220), calls=%async_computation.3 | async-start | bytes 786432 | tf_op jit(solution)/shard_map/all_to_all | solution.py:97
  98.2 1.5 scatter_custom_fusion.1
  99.8 0.1 copy.41
  100.0 1.5 scatter_custom_fusion
  101.5 0.1 copy.40
  101.8 0.2 copy.46
  102.0 1.2 gather_fusion.2
  103.2 0.2 reshape.227
  103.3 2.1 %gather_fusion.3 = bf16[128,2,768]{2,1,0:T(2,128)(2,1)} fusion(bf16[128,2,768]{2,1,0:T(2,128)(2,1)S(1)} %reshape.227, s32[1024]{0:T(1024)S(1)} %pad_clamp_fusion), kind=kCustom, calls=%fused_computation.3 | custom fusion | bytes 786944 | tf_op jit(solution)/shard_map/gather | solution.py:139
  105.4 10.5 %all-to-all-done.3 = bf16[128,2,768]{2,1,0:T(2,128)(2,1)S(1)} async-done(((bf16[128,2,768]{2,1,0:T(2,128)(2,1)}), bf16[128,2,768]{2,1,0:T(2,128)(2,1)S(1)}, u32[]{:S(2)}, u32[]{:S(2)}) %all-to-all-start.3) | async-done | bytes 393248 | tf_op jit(solution)/shard_map/all_to_all | solution.py:97
  116.0 6.2 %all-to-all-start.6 = ((s32[128,1,1]{2,1,0:T(1,128)}), s32[128,1,1]{2,1,0:T(1,128)S(1)}, u32[]{:S(2)}, u32[]{:S(2)}) async-start(s32[128,1,1]{2,1,0:T(1,128)} %copy.45), calls=%async_computation.6 | async-start | bytes 131072 | tf_op jit(solution)/shard_map/all_to_all | solution.py:140
  122.1 0.1 reshape.285
  122.3 1.7 scatter_custom_fusion.2
  124.0 0.2 copy.42
  124.2 0.1 subtract_convert_fusion
  124.3 9.0 %all-to-all-done.6 = s32[128,1,1]{2,1,0:T(1,128)S(1)} async-done(((s32[128,1,1]{2,1,0:T(1,128)}), s32[128,1,1]{2,1,0:T(1,128)S(1)}, u32[]{:S(2)}, u32[]{:S(2)}) %all-to-all-start.6) | async-done | bytes 544 | tf_op jit(solution)/shard_map/all_to_all | solution.py:140
  133.4 6.4 %all-to-all-start.7 = ((bf16[128,2,768]{2,1,0:T(2,128)(2,1)}), bf16[128,2,768]{2,1,0:T(2,128)(2,1)S(1)}, u32[]{:S(2)}, u32[]{:S(2)}) async-start(bf16[128,2,768]{2,1,0:T(2,128)(2,1)} %gather_fusion.3), calls=%async_computation.7 | async-start | bytes 786432 | tf_op jit(solution)/shard_map/all_to_all | solution.py:139
  139.8 4.2 %while.11 = (s32[]{:T(128)}, bf16[4,256,2,96]{1,3,2,0:T(8,128)(2,1)S(1)}, bf16[4,256,96]{1,2,0:T(8,128)(2,1)S(1)}, bf16[4,256,96]{1,2,0:T(8,128)(2,1)S(1)}, bf16...) while((s32[]{:T(128)}, ...), condition=%wide.region_8.9_spmd.clone, body=%wide.region_5.8_spmd.clone.sunk | while | flops 76874752 | bytes 2319445 | solution.py:72
  139.9 0.3 fusion.63
  140.1 0.4 fusion.62
  140.5 0.3 fusion.64
  140.9 0.3 fusion.63
  141.2 0.4 fusion.62
  141.6 0.3 fusion.64
  142.0 0.3 fusion.63
  142.2 0.4 fusion.62
  142.6 0.3 fusion.64
  143.0 0.3 fusion.63
  143.3 0.4 fusion.62
  143.7 0.3 fusion.64
  143.9 0.2 copy.43
  144.1 1.2 gather_fusion.1
  145.3 0.9 reshape.224
  146.2 11.2 %all-to-all-done.7 = bf16[128,2,768]{2,1,0:T(2,128)(2,1)S(1)} async-done(((bf16[128,2,768]{2,1,0:T(2,128)(2,1)}), bf16[128,2,768]{2,1,0:T(2,128)(2,1)S(1)}, u32[]{:S(2)}, u32[]{:S(2)}) %all-to-all-start.7) | async-done | bytes 393248 | tf_op jit(solution)/shard_map/all_to_all | solution.py:139
  157.4 6.2 %all-to-all-start.4 = ((bf16[128,2,768]{2,1,0:T(2,128)(2,1)}), bf16[128,2,768]{2,1,0:T(2,128)(2,1)S(1)}, u32[]{:S(2)}, u32[]{:S(2)}) async-start(bf16[128,2,768]{2,1,0:T(2,128)(2,1)} %reshape.224), calls=%async_computation.4 | async-start | bytes 786432 | tf_op jit(solution)/shard_map/all_to_all | solution.py:131
  163.6 2.4 %reduce.4 = s32[128]{0:T(128)S(1)} reduce(s32[128,1,1]{2,1,0:T(1,128)S(1)} %all-to-all-done.6, s32[]{:T(128)} %constant.11.clone.1), dimensions={1,2}, to_apply=%all_to_all.44.reduce_sub_computation | reduce | bytes 1028 | tf_op jit(solution)/shard_map/all_to_all | solution.py:140
  165.9 0.2 broadcast_in_dim.21
  166.1 4.4 %scatter_fusion = bf16[128,2,768]{2,1,0:T(2,128)(2,1)S(1)} fusion(bf16[128,2,768]{2,1,0:T(2,128)(2,1)S(1)} %broadcast_in_dim.21, s32[128]{0:T(128)S(1)} %fusion.37, bf16[128,2,768]{2,1,0:T(2,128)(2,1)S(1)} %all-to-all-done.7), kind=kCustom, calls=%fused_computation.7 | custom fusion | bytes 1180160 | tf_op jit(solution)/shard_map/scatter | solution.py:147
  170.5 0.9 reshape.228
  171.4 10.0 %all-to-all-done.4 = bf16[128,2,768]{2,1,0:T(2,128)(2,1)S(1)} async-done(((bf16[128,2,768]{2,1,0:T(2,128)(2,1)}), bf16[128,2,768]{2,1,0:T(2,128)(2,1)S(1)}, u32[]{:S(2)}, u32[]{:S(2)}) %all-to-all-start.4) | async-done | bytes 393248 | tf_op jit(solution)/shard_map/all_to_all | solution.py:131
  181.4 0.9 reshape.225
  (37 shorter events, 1.2 us)
Async XLA Ops:
  0.6 0.7 copy-start.5
  1.3 19.4 %copy-start.4 = (s32[256]{0:T(256)S(1)}, s32[256]{0:T(256)}, u32[]{:S(2)}) copy-start(s32[256]{0:T(256)} %param.11) | copy-start | bytes 3076
  2.0 18.0 %copy-start = (s32[1,256]{1,0:T(1,128)S(1)}, s32[1,256]{1,0:T(1,128)}, u32[]{:S(2)}) copy-start(s32[1,256]{1,0:T(1,128)} %param.12) | copy-start | bytes 3076
  2.0 35.3 %copy-start.2 = (bf16[256,384]{1,0:T(8,128)(2,1)S(1)}, bf16[256,384]{1,0:T(8,128)(2,1)}, u32[]{:S(2)}) copy-start(bf16[256,384]{1,0:T(8,128)(2,1)} %param.9) | copy-start | bytes 589828
  2.0 29.1 %all-to-all-start.5 = ((s32[128,1,1]{2,1,0:T(1,128)}), s32[128,1,1]{2,1,0:T(1,128)S(1)}, u32[]{:S(2)}, u32[]{:S(2)}) async-start(s32[128,1,1]{2,1,0:T(1,128)} %copy.44), calls=%async_computation.5 | async-start | bytes 131072 | tf_op jit(solution)/shard_map/all_to_all | solution.py:119
  31.1 17.3 %all-to-all-start = ((s32[128,1,2]{2,1,0:T(1,128)}), s32[128,1,2]{2,1,0:T(1,128)S(1)}, u32[]{:S(2)}, u32[]{:S(2)}) async-start(s32[128,1,2]{2,1,0:T(1,128)} %bitcast), calls=%async_computation | async-start | bytes 131072 | tf_op jit(solution)/shard_map/all_to_all | solution.py:118
  37.4 17.3 %copy-start.1 = (bf16[256,768]{1,0:T(8,128)(2,1)S(1)}, bf16[256,768]{1,0:T(8,128)(2,1)}, u32[]{:S(2)}) copy-start(bf16[256,768]{1,0:T(8,128)(2,1)} %param.8) | copy-start | bytes 1179652
  48.5 19.9 %all-to-all-start.2 = ((bf16[128,2,384]{2,1,0:T(2,128)(2,1)}), bf16[128,2,384]{2,1,0:T(2,128)(2,1)S(1)}, u32[]{:S(2)}, u32[]{:S(2)}) async-start(bf16[128,2,384]{2,1,0:T(2,128)(2,1)} %reshape.215), calls=%async_computation.2 | async-start | bytes 393216 | tf_op jit(solution)/shard_map/all_to_all | solution.py:104
  54.7 0.9 copy-start.3
  68.4 23.4 %all-to-all-start.1 = ((bf16[128,2,384]{2,1,0:T(2,128)(2,1)}), bf16[128,2,384]{2,1,0:T(2,128)(2,1)S(1)}, u32[]{:S(2)}, u32[]{:S(2)}) async-start(bf16[128,2,384]{2,1,0:T(2,128)(2,1)} %reshape.212), calls=%async_computation.1 | async-start | bytes 393216 | tf_op jit(solution)/shard_map/all_to_all | solution.py:111
  91.7 24.2 %all-to-all-start.3 = ((bf16[128,2,768]{2,1,0:T(2,128)(2,1)}), bf16[128,2,768]{2,1,0:T(2,128)(2,1)S(1)}, u32[]{:S(2)}, u32[]{:S(2)}) async-start(bf16[128,2,768]{2,1,0:T(2,128)(2,1)} %reshape.220), calls=%async_computation.3 | async-start | bytes 786432 | tf_op jit(solution)/shard_map/all_to_all | solution.py:97
  116.0 17.4 %all-to-all-start.6 = ((s32[128,1,1]{2,1,0:T(1,128)}), s32[128,1,1]{2,1,0:T(1,128)S(1)}, u32[]{:S(2)}, u32[]{:S(2)}) async-start(s32[128,1,1]{2,1,0:T(1,128)} %copy.45), calls=%async_computation.6 | async-start | bytes 131072 | tf_op jit(solution)/shard_map/all_to_all | solution.py:140
  133.4 24.0 %all-to-all-start.7 = ((bf16[128,2,768]{2,1,0:T(2,128)(2,1)}), bf16[128,2,768]{2,1,0:T(2,128)(2,1)S(1)}, u32[]{:S(2)}, u32[]{:S(2)}) async-start(bf16[128,2,768]{2,1,0:T(2,128)(2,1)} %gather_fusion.3), calls=%async_computation.7 | async-start | bytes 786432 | tf_op jit(solution)/shard_map/all_to_all | solution.py:139
  157.4 24.0 %all-to-all-start.4 = ((bf16[128,2,768]{2,1,0:T(2,128)(2,1)}), bf16[128,2,768]{2,1,0:T(2,128)(2,1)S(1)}, u32[]{:S(2)}, u32[]{:S(2)}) async-start(bf16[128,2,768]{2,1,0:T(2,128)(2,1)} %reshape.224), calls=%async_computation.4 | async-start | bytes 786432 | tf_op jit(solution)/shard_map/all_to_all | solution.py:131
where the time goes:
time: 183 us; the launch traced here: 182 us
  waiting for transfers between devices  78.1 us (43%)
  starting transfers between devices  65 us (36%)
  local copies, waits for them, and re-layouts  25.4 us (14%)
  other arithmetic  9.05 us (5%)
  matrix products  3.62 us (2%)
    all_to_all x1, starting transfers between devices, per_device(): lax.all_to_all(owner_column, 'dev', split_axis=0, concat_axis=0, tiled=True)  17.9 us
    all_to_all x1, waiting for transfers between devices, per_device(): lax.all_to_all(values.reshape(device_count, page_rows, key_width), 'dev',...  13.4 us
    all_to_all x1, waiting for transfers between devices, per_device(): lax.all_to_all(stored[owner_order], 'dev', split_axis=0, concat_axis=0, t...  11.2 us
    all_to_all x1, waiting for transfers between devices, per_device(): lax.all_to_all(queries.reshape(device_count, page_rows, query_width), 'de...  10.5 us
    all_to_all x1, waiting for transfers between devices, per_device(): lax.all_to_all(grouped_index, 'dev', split_axis=0, concat_axis=0, tiled=T...  10.4 us
    all_to_all x1, waiting for transfers between devices, per_device(): lax.all_to_all(going_back, 'dev', split_axis=0, concat_axis=0, tiled=True)  9.97 us
    all_to_all x1, starting transfers between devices, per_device(): lax.all_to_all(values.reshape(device_count, page_rows, key_width), 'dev',...  9.65 us
    all_to_all x1, waiting for transfers between devices, per_device(): lax.all_to_all(owner_column, 'dev', split_axis=0, concat_axis=0, tiled=True)  9.65 us
  transfers between devices with their start and end apart: 8, of which 8 were waited for; matrix products, arithmetic and copies ran while one was open for 19% of the time, Pallas kernels for 0%

commit v1 on v0

v1 whole, which is shorter than its diff:
```python
import math

import jax
import jax.numpy as jnp
from jax import lax
from jax.sharding import PartitionSpec as P

QUERY_HEAD_COUNT = 8
KEY_VALUE_HEADS = 4


ROPE_BASE = 100000.0
NEG_FILL = -1e30


def positions_of(request_labels):
    row_width = request_labels.shape[0]
    counter = jnp.arange(row_width, dtype=jnp.int32)
    boundary = jnp.concatenate(
        [jnp.ones((1,), jnp.bool_), request_labels[1:] != request_labels[:-1]]
    )
    starts = lax.cummax(jnp.where(boundary, counter, jnp.zeros_like(counter)), axis=0)
    return counter - starts


def apply_rotary(features, token_positions, head_count):
    head_depth = features.shape[1] // head_count
    half_depth = head_depth // 2
    freqs = ROPE_BASE ** (-2.0 * jnp.arange(half_depth, dtype=jnp.float32) / head_depth)
    angles = token_positions.astype(jnp.float32)[:, None] * freqs[None, :]
    cosine = jnp.cos(angles)[:, None, :]
    sine = jnp.sin(angles)[:, None, :]
    split_heads = features.astype(jnp.float32).reshape(features.shape[0], head_count, head_depth)
    first = split_heads[..., :half_depth]
    second = split_heads[..., half_depth:]
    turned = jnp.concatenate(
        [first * cosine - second * sine, second * cosine + first * sine], axis=-1
    )
    return turned.reshape(features.shape).astype(jnp.bfloat16)


def attend(query_turned, key_turned, value_matrix, allowed, kv_heads):
    rows = query_turned.shape[0]
    head_depth = key_turned.shape[1] // kv_heads
    group_size = query_turned.shape[1] // (kv_heads * head_depth)
    q = query_turned.reshape(rows, kv_heads, group_size, head_depth)
    k = key_turned.reshape(rows, kv_heads, head_depth)
    v = value_matrix.reshape(rows, kv_heads, head_depth)
    logits = jnp.einsum("jhgd,khd->hgjk", q, k, preferred_element_type=jnp.float32)
    logits = logits * (1.0 / math.sqrt(head_depth))
    logits = jnp.where(allowed[None, None], logits, NEG_FILL)
    highest = jnp.max(logits, axis=-1, keepdims=True)
    expo = jnp.exp(logits - highest)
    weights = (expo / jnp.sum(expo, axis=-1, keepdims=True)).astype(jnp.bfloat16)
    out = jnp.einsum("hgjk,khe->jhge", weights, v, preferred_element_type=jnp.float32)
    return out.reshape(rows, -1).astype(jnp.bfloat16)


def row_permute(matrix, target_rows):
    rows = matrix.shape[0]
    onehot = (jnp.arange(rows, dtype=jnp.int32)[:, None] == target_rows[None, :]).astype(
        matrix.dtype
    )
    return jnp.dot(onehot, matrix, preferred_element_type=jnp.float32).astype(matrix.dtype)


def per_device(queries, keys, values, deal_index, segments, page_owner):
    device_count = lax.axis_size("dev")
    row_count = queries.shape[0]
    page_rows = row_count // device_count
    query_width = queries.shape[1]
    key_width = keys.shape[1]
    request_labels = segments[0]
    dealt_positions = positions_of(request_labels)

    arrival_rows = jnp.arange(row_count, dtype=jnp.int32)
    local_dealt = deal_index % row_count
    row_owner = page_owner[0][arrival_rows // page_rows]
    meta = jnp.stack([local_dealt, row_owner], axis=1).astype(jnp.bfloat16)
    outgoing = jnp.concatenate([queries, keys, values, meta], axis=1)
    width = outgoing.shape[1]
    received = lax.all_to_all(
        outgoing.reshape(device_count, page_rows, width), "dev", split_axis=0, concat_axis=0, tiled=True
    ).reshape(row_count, width)

    q_in = received[:, :query_width]
    k_in = received[:, query_width : query_width + key_width]
    v_in = received[:, query_width + key_width : query_width + 2 * key_width]
    dealt_row = received[:, query_width + 2 * key_width].astype(jnp.int32)
    owner_in = received[:, query_width + 2 * key_width + 1].astype(jnp.int32)

    request_in = request_labels[dealt_row]
    position_in = dealt_positions[dealt_row]
    allowed = (request_in[:, None] == request_in[None, :]) & (dealt_row[None, :] <= dealt_row[:, None])

    key_turned = apply_rotary(k_in, position_in, KEY_VALUE_HEADS)
    query_turned = apply_rotary(q_in, position_in, QUERY_HEAD_COUNT)
    output_rows = attend(query_turned, key_turned, v_in, allowed, KEY_VALUE_HEADS)

    source_device = (arrival_rows // page_rows).astype(jnp.bfloat16)[:, None]
    stored = jnp.concatenate([key_turned, v_in, source_device], axis=1)
    stored_for_owner = row_permute(stored, owner_in * page_rows + arrival_rows % page_rows)
    going_back = jnp.concatenate([output_rows, stored_for_owner], axis=1)
    back_width = going_back.shape[1]
    returned = lax.all_to_all(
        going_back.reshape(device_count, page_rows, back_width),
        "dev",
        split_axis=0,
        concat_axis=0,
        tiled=True,
    ).reshape(row_count, back_width)

    attended = returned[:, :query_width]
    cache_in = returned[:, query_width : query_width + 2 * key_width]
    cache_source = returned[:, query_width + 2 * key_width].astype(jnp.int32)
    cache = row_permute(cache_in, cache_source * page_rows + arrival_rows % page_rows)
    return (attended, cache)


def solution(mesh):
    in_specs = (
        P(("grp", "dev"), None),
        P(("grp", "dev"), None),
        P(("grp", "dev"), None),
        P(("grp", "dev")),
        P(("grp", "dev"), None),
        P(("grp", "dev"), None),
    )
    out_specs = (P(("grp", "dev"), None), P(("grp", "dev"), None))
    return jax.shard_map(
        per_device, mesh=mesh, in_specs=in_specs, out_specs=out_specs, check_vma=False
    )
```

time: 183 us -> 99.3 us (0.54)
  waiting for transfers between devices: 78.1 us -> 26.4 us
  starting transfers between devices: 65 us -> 17.8 us
  blocking collectives: 0 us -> 32.9 us
  local copies, waits for them, and re-layouts: 25.4 us -> 13.1 us
  other arithmetic: 9.05 us -> 2.57 us
  matrix products: 3.62 us -> 5.46 us
    all_to_all x8 -> x1, waiting for transfers between devices: 78.1 us -> 26.4 us  [per_device(): lax.all_to_all(outgoing.reshape(device_count, page_rows, width), 'dev', s...]
    all_to_all x8 -> x1, starting transfers between devices: 65 us -> 17.8 us  [per_device(): lax.all_to_all(outgoing.reshape(device_count, page_rows, width), 'dev', s...]
    all_to_all x0 -> x1, blocking collectives: none -> 32.9 us  [per_device(): lax.all_to_all(going_back.reshape(device_count, page_rows, back_width), '...]
    scatter x5 -> x0, local copies, waits for them, and re-layouts: 9.32 us -> none  [the longest x4 4.93 us: place(): jnp.zeros((row_count, received.shape[-1]), received.dtype).at[local_rows]]
    all_to_all x2 -> x0, other arithmetic: 4.7 us -> none  [the longest x1 2.35 us: per_device(): lax.all_to_all(owner_column, 'dev', split_axis=0, concat_axis=0, tiled=True)]
    reshape x10 -> x4, local copies, waits for them, and re-layouts: 5.52 us -> 2.86 us  [the longest x1 1.23 us: per_device(): outgoing.reshape(device_count, page_rows, width)]
    sort x1 -> x0, other arithmetic: 2.61 us -> none  [per_device(): owner_order = jnp.argsort(arrived_owner.reshape(-1))]
    all_to_all x3 -> x0, local copies, waits for them, and re-layouts: 2.24 us -> none  [the longest x1 0.77 us: per_device(): lax.all_to_all(grouped_index, 'dev', split_axis=0, concat_axis=0, tiled=T...]
  transfers between devices with their start and end apart: 8 -> 1, of which waited for: 8 -> 1; matrix products, arithmetic and copies ran while one was open for 19% -> 1% of each run, Pallas kernels for 0% -> 0%
where the time goes in v1:
time: 99.3 us; the launch traced here: 99 us
  blocking collectives  32.9 us (33%)
  waiting for transfers between devices  26.4 us (27%)
  starting transfers between devices  17.8 us (18%)
  local copies, waits for them, and re-layouts  13.1 us (13%)
  matrix products  5.46 us (5%)
  other arithmetic  2.57 us (3%)
    all_to_all x1, blocking collectives, per_device(): lax.all_to_all(going_back.reshape(device_count, page_rows, back_width), '...  32.9 us
    all_to_all x1, waiting for transfers between devices, per_device(): lax.all_to_all(outgoing.reshape(device_count, page_rows, width), 'dev', s...  26.4 us
    all_to_all x1, starting transfers between devices, per_device(): lax.all_to_all(outgoing.reshape(device_count, page_rows, width), 'dev', s...  17.8 us
    sub x1, matrix products, attend(): expo = jnp.exp(logits - highest)  2.21 us
  transfers between devices with their start and end apart: 1, of which 1 were waited for; matrix products, arithmetic and copies ran while one was open for 1% of the time, Pallas kernels for 0%

profile of v1, /device:TPU:6, one launch (start us, length us, event | category | flops | bytes accessed | tf_op | source)
XLA Modules:
  0.0 99.0 jit_solution(15777706964415757615)
XLA Ops:
  0.6 0.0 copy-start
  0.6 0.1 fusion.20
  0.8 0.5 copy-done
  1.3 1.9 %gather_fusion = s32[256]{0:T(256)S(1)} fusion(s32[128]{0:T(128)S(1)} %bitcast.42, s32[1024]{0:T(1024)S(1)} %pad_clamp_fusion.1), kind=kCustom, calls=%fused_computation | custom fusion | bytes 3072 | tf_op jit(solution)/shard_map/gather | solution.py:78
  3.2 0.1 stack.13
  3.3 0.7 fusion.27
  4.0 0.1 stack.12
  4.1 1.4 %concatenate.22 = bf16[256,1538]{1,0:T(8,128)(2,1)S(1)} concatenate(bf16[256,768]{1,0:T(8,128)(2,1)} %param.6, bf16[256,384]{1,0:T(8,128)(2,1)} %param.7, bf16[256,384]{1,0:T(8,128)(2,1)} %param.8, bf16[256,1]{1,0:T(8,128)(2,1)S(1)} %stack.12, bf16[256,1]{1,0:T(8,128)(2,1)S(1)} %stack.13), dimensions={1} | concatenate | bytes 1574912 | tf_op jit(solution)/shard_map/concatenate | solution.py:80
  5.4 0.0 copy-start.1
  5.5 1.2 %reshape.256 = bf16[128,2,1538]{2,1,0:T(2,128)(2,1)} reshape(bf16[256,1538]{1,0:T(8,128)(2,1)S(1)} %concatenate.22) | data formatting | bytes 1574912 | tf_op jit(solution)/shard_map/reshape | solution.py:83
  6.7 17.8 %all-to-all-start = ((bf16[128,2,1538]{2,1,0:T(2,128)(2,1)}), bf16[128,2,1538]{2,1,0:T(2,128)(2,1)S(1)}, u32[]{:S(2)}, u32[]{:S(2)}) async-start(bf16[128,2,1538]{2,1,0:T(2,128)(2,1)} %reshape.256), calls=%async_computation | async-start | bytes 1703936 | tf_op jit(solution)/shard_map/all_to_all | solution.py:82
  24.5 0.0 copy-done.1
  24.5 0.1 compare_reduce_fusion
  24.6 0.1 fusion.25
  24.7 0.3 reduce-window.9
  25.0 0.1 slice.57
  25.1 0.1 slice_reduce_fusion
  25.3 0.1 bitcast_subtract_fusion
  25.3 26.4 %all-to-all-done = bf16[128,2,1538]{2,1,0:T(2,128)(2,1)S(1)} async-done(((bf16[128,2,1538]{2,1,0:T(2,128)(2,1)}), bf16[128,2,1538]{2,1,0:T(2,128)(2,1)S(1)}, u32[]{:S(2)}, u32[]{:S(2)}) %all-to-all-start) | async-done | bytes 787488 | tf_op jit(solution)/shard_map/all_to_all | solution.py:82
  51.7 0.6 reshape.257
  52.4 0.2 convert_reduce_fusion
  52.6 0.1 slice_convert_fusion
  52.7 1.9 %gather_fusion.2 = s32[256]{0:T(256)S(1)} fusion(s32[256]{0:T(256)S(1)} %bitcast_subtract_fusion, s32[1024]{0:T(1024)S(1)} %pad_clamp_fusion), kind=kCustom, calls=%fused_computation.2 | custom fusion | bytes 3072 | tf_op jit(solution)/shard_map/gather | solution.py:93
  54.7 0.3 copy.19
  55.0 0.2 copy.18
  55.1 0.3 multiply_cosine_fusion
  55.4 0.1 subtract_convert_fusion
  55.5 0.1 multiply_subtract_fusion
  55.6 1.9 %gather_fusion.1 = s32[256]{0:T(256)S(1)} fusion(s32[256]{0:T(256)S(1)} %bitcast.43, s32[1024]{0:T(1024)S(1)} %pad_clamp_fusion), kind=kCustom, calls=%fused_computation.1 | custom fusion | bytes 3072 | tf_op jit(solution)/shard_map/gather | solution.py:92
  57.5 0.1 copy.17
  57.7 0.2 copy.21
  57.9 0.1 compare_and_fusion
  58.1 2.2 %fusion.35 = (f32[4,2,256]{2,1,0:T(2,128)S(1)}, f32[4,2,256,256]{2,3,1,0:T(8,128)}) fusion(pred[256,256]{0,1:T(8,128)(4,1)S(1)} %compare_and_fusion, bf16[256,4,2,96]{0,3,2,1:T(8,128)(2,1)S(1)} %bitcast.47, bf16[256,4,48]{0,2,1:T(8,128)(2,1)S(1)} %get-tuple-element.10, bf16[256,4,48]{0,2,1:T(8,128)(2,1)S(1)} %get-tuple-element.9), kind=kOutput, calls=%fused_computation.72 | convolution fusion | flops 103153920 | bytes 2760704 | tf_op jit(solution)/shard_map/sub | solution.py:53
  60.3 1.9 %convolution_convert_fusion.2 = bf16[4,96,2,256]{3,1,2,0:T(8,128)(2,1)S(1)} fusion(bf16[256,4,96,1]{0,2,3,1:T(8,128)(2,1)S(1)} %bitcast.49, f32[4,2,256,256]{2,3,1,0:T(8,128)} %get-tuple-element.14, f32[4,2,256]{2,1,0:T(2,128)S(1)} %get-tuple-element.13), kind=kOutput, calls=%fused_computation.10 | convolution fusion | flops 101908480 | bytes 2695168 | tf_op jit(solution)/shard_map/hgjk,khe->jhge/dot_general | solution.py:55
  62.2 0.3 convolution_convert_fusion
  62.5 0.1 pad_maximum_fusion
  62.6 0.7 copy.22
  63.3 0.3 reshape.264
  63.6 32.9 %all_to_all.10 = bf16[128,2,1537]{2,1,0:T(2,128)(2,1)S(1)} all-to-all(bf16[128,2,1537]{2,1,0:T(2,128)(2,1)S(1)} %reshape.264), channel_id=1, replica_groups=mesh['grp'=4,'dev'=128] {'dev'}, dimensions={0} | all-to-all | bytes 1573888 | tf_op jit(solution)/shard_map/all_to_all | solution.py:105
  96.5 0.6 reshape.265
  97.1 0.1 multiply_reduce_fusion
  97.2 0.8 slice.82
  98.0 1.0 %convolution_convert_fusion.1 = bf16[256,768]{1,0:T(8,128)(2,1)} fusion(bf16[256,1537]{1,0:T(8,128)(2,1)S(1)} %reshape.265, s32[256]{0:T(256)S(1)} %fusion.28), kind=kOutput, calls=%fused_computation.9 | convolution fusion | flops 100925440 | bytes 787456 | tf_op jit(solution)/shard_map/dot_general | solution.py:64
  (12 shorter events, 0.2 us)
Async XLA Ops:
  0.6 0.7 copy-start
  5.4 19.1 %copy-start.1 = (s32[1,256]{1,0:T(1,128)S(1)}, s32[1,256]{1,0:T(1,128)}, u32[]{:S(2)}) copy-start(s32[1,256]{1,0:T(1,128)} %param.10) | copy-start | bytes 3076
  6.7 45.0 %all-to-all-start = ((bf16[128,2,1538]{2,1,0:T(2,128)(2,1)}), bf16[128,2,1538]{2,1,0:T(2,128)(2,1)S(1)}, u32[]{:S(2)}, u32[]{:S(2)}) async-start(bf16[128,2,1538]{2,1,0:T(2,128)(2,1)} %reshape.256), calls=%async_computation | async-start | bytes 1703936 | tf_op jit(solution)/shard_map/all_to_all | solution.py:82

commit v2 on v1

--- a/solution.py
+++ b/solution.py
@@ -64,6 +64,19 @@
     return jnp.dot(onehot, matrix, preferred_element_type=jnp.float32).astype(matrix.dtype)
 
 
+def one_hot_take(table, index):
+    return jnp.sum(
+        jnp.where(index[:, None] == jnp.arange(table.shape[0], dtype=jnp.int32)[None, :], table[None, :], 0),
+        axis=1,
+    )
+
+
+def row_take(matrix, source_rows):
+    rows = matrix.shape[0]
+    onehot = (source_rows[:, None] == jnp.arange(rows, dtype=jnp.int32)[None, :]).astype(matrix.dtype)
+    return jnp.dot(onehot, matrix, preferred_element_type=jnp.float32).astype(matrix.dtype)
+
+
 def per_device(queries, keys, values, deal_index, segments, page_owner):
     device_count = lax.axis_size("dev")
     row_count = queries.shape[0]
@@ -74,46 +87,46 @@
     dealt_positions = positions_of(request_labels)
 
     arrival_rows = jnp.arange(row_count, dtype=jnp.int32)
+    devices = jnp.arange(device_count, dtype=jnp.int32)
+    owner_row = page_owner[0]
+    page_of_owner = jnp.sum(
+        jnp.where(owner_row[None, :] == devices[:, None], devices[None, :], 0), axis=1
+    )
     local_dealt = deal_index % row_count
-    row_owner = page_owner[0][arrival_rows // page_rows]
-    meta = jnp.stack([local_dealt, row_owner], axis=1).astype(jnp.bfloat16)
+    page_meta = jnp.where(
+        arrival_rows % page_rows == 0,
+        jnp.repeat(owner_row, page_rows),
+        jnp.repeat(page_of_owner, page_rows),
+    )
+    meta = jnp.stack([local_dealt, page_meta], axis=1).astype(jnp.bfloat16)
     outgoing = jnp.concatenate([queries, keys, values, meta], axis=1)
-    width = outgoing.shape[1]
-    received = lax.all_to_all(
-        outgoing.reshape(device_count, page_rows, width), "dev", split_axis=0, concat_axis=0, tiled=True
-    ).reshape(row_count, width)
+    received = lax.all_to_all(outgoing, "dev", split_axis=0, concat_axis=0, tiled=True)
 
     q_in = received[:, :query_width]
     k_in = received[:, query_width : query_width + key_width]
     v_in = received[:, query_width + key_width : query_width + 2 * key_width]
     dealt_row = received[:, query_width + 2 * key_width].astype(jnp.int32)
-    owner_in = received[:, query_width + 2 * key_width + 1].astype(jnp.int32)
+    page_meta_in = received[:, query_width + 2 * key_width + 1].astype(jnp.int32)
+    paired = page_meta_in.reshape(device_count, page_rows)
+    owner_in = jnp.repeat(paired[:, 0], page_rows)
+    page_from = jnp.repeat(paired[:, 1], page_rows)
 
-    request_in = request_labels[dealt_row]
-    position_in = dealt_positions[dealt_row]
+    request_in = one_hot_take(request_labels, dealt_row)
+    position_in = one_hot_take(dealt_positions, dealt_row)
     allowed = (request_in[:, None] == request_in[None, :]) & (dealt_row[None, :] <= dealt_row[:, None])
 
     key_turned = apply_rotary(k_in, position_in, KEY_VALUE_HEADS)
     query_turned = apply_rotary(q_in, position_in, QUERY_HEAD_COUNT)
     output_rows = attend(query_turned, key_turned, v_in, allowed, KEY_VALUE_HEADS)
 
-    source_device = (arrival_rows // page_rows).astype(jnp.bfloat16)[:, None]
-    stored = jnp.concatenate([key_turned, v_in, source_device], axis=1)
+    stored = jnp.concatenate([key_turned, v_in], axis=1)
     stored_for_owner = row_permute(stored, owner_in * page_rows + arrival_rows % page_rows)
     going_back = jnp.concatenate([output_rows, stored_for_owner], axis=1)
-    back_width = going_back.shape[1]
-    returned = lax.all_to_all(
-        going_back.reshape(device_count, page_rows, back_width),
-        "dev",
-        split_axis=0,
-        concat_axis=0,
-        tiled=True,
-    ).reshape(row_count, back_width)
+    returned = lax.all_to_all(going_back, "dev", split_axis=0, concat_axis=0, tiled=True)
 
     attended = returned[:, :query_width]
-    cache_in = returned[:, query_width : query_width + 2 * key_width]
-    cache_source = returned[:, query_width + 2 * key_width].astype(jnp.int32)
-    cache = row_permute(cache_in, cache_source * page_rows + arrival_rows % page_rows)
+    cache_in = returned[:, query_width:]
+    cache = row_take(cache_in, page_from * page_rows + arrival_rows % page_rows)
     return (attended, cache)
 
 

time: 99.3 us -> 91.6 us (0.922)
  blocking collectives: 32.9 us -> 0 us
  waiting for transfers between devices: 26.4 us -> 52 us
  starting transfers between devices: 17.8 us -> 24 us
  local copies, waits for them, and re-layouts: 13.1 us -> 8.53 us
  matrix products: 5.46 us -> 2.53 us
    all_to_all x1 -> x0, blocking collectives: 32.9 us -> none  [per_device(): lax.all_to_all(going_back.reshape(device_count, page_rows, back_width), '...]
    all_to_all x1 -> x2, waiting for transfers between devices: 26.4 us -> 52 us  [the longest x1 26.4 us: per_device(): lax.all_to_all(outgoing, 'dev', split_axis=0, concat_axis=0, tiled=True)]
    all_to_all x1 -> x2, starting transfers between devices: 17.8 us -> 24 us  [the longest x1 17.8 us: per_device(): lax.all_to_all(outgoing, 'dev', split_axis=0, concat_axis=0, tiled=True)]
    gather x3 -> x0, local copies, waits for them, and re-layouts: 5.77 us -> none  [the longest x1 1.95 us: per_device(): position_in = dealt_positions[dealt_row]]
    all_to_all x0 -> x4, local copies, waits for them, and re-layouts: none -> 3.35 us  [the longest x2 1.88 us: per_device(): lax.all_to_all(outgoing, 'dev', split_axis=0, concat_axis=0, tiled=True)]
    reshape x4 -> x2, local copies, waits for them, and re-layouts: 2.86 us -> 0.31 us  [the longest x1 0.16 us: per_device(): jnp.repeat(page_of_owner, page_rows)]
    dot_general x1, matrix products: 1.91 us -> 0.32 us  [attend(): jnp.einsum('hgjk,khe->jhge', weights, v, preferred_element_type=jnp.float32)]
    sub x1, matrix products: 2.21 us -> 0.89 us  [attend(): expo = jnp.exp(logits - highest)]
  transfers between devices with their start and end apart: 1 -> 2, of which waited for: 1 -> 2; matrix products, arithmetic and copies ran while one was open for 1% -> 1% of each run, Pallas kernels for 0% -> 0%
where the time goes in v2:
time: 91.6 us; the launch traced here: 91.3 us
  waiting for transfers between devices  52 us (57%)
  starting transfers between devices  24 us (26%)
  local copies, waits for them, and re-layouts  8.53 us (9%)
  other arithmetic  3.39 us (4%)
  matrix products  2.53 us (3%)
    all_to_all x1, waiting for transfers between devices, per_device(): lax.all_to_all(outgoing, 'dev', split_axis=0, concat_axis=0, tiled=True)  26.4 us
    all_to_all x1, waiting for transfers between devices, per_device(): lax.all_to_all(going_back, 'dev', split_axis=0, concat_axis=0, tiled=True)  25.6 us
    all_to_all x1, starting transfers between devices, per_device(): lax.all_to_all(outgoing, 'dev', split_axis=0, concat_axis=0, tiled=True)  17.8 us
    all_to_all x1, starting transfers between devices, per_device(): lax.all_to_all(going_back, 'dev', split_axis=0, concat_axis=0, tiled=True)  6.18 us
    all_to_all x2, local copies, waits for them, and re-layouts, per_device(): lax.all_to_all(outgoing, 'dev', split_axis=0, concat_axis=0, tiled=True)  1.88 us
  transfers between devices with their start and end apart: 2, of which 2 were waited for; matrix products, arithmetic and copies ran while one was open for 1% of the time, Pallas kernels for 0%

profile of v2, /device:TPU:6, one launch (start us, length us, event | category | flops | bytes accessed | tf_op | source)
XLA Modules:
  0.0 91.3 jit_solution(3281733469554108800)
XLA Ops:
  0.6 0.8 select_reduce_fusion.2
  1.4 0.1 broadcast_in_dim.85
  1.5 0.2 reshape.269
  1.6 0.7 broadcast_in_dim.52
  2.4 0.1 reshape.268
  2.5 0.1 copy.29
  2.7 0.7 fusion.21
  3.4 0.1 stack.8
  3.5 1.4 %concatenate.22 = bf16[256,1538]{1,0:T(8,128)(2,1)S(1)} concatenate(bf16[256,768]{1,0:T(8,128)(2,1)} %param.6, bf16[256,384]{1,0:T(8,128)(2,1)} %param.7, bf16[256,384]{1,0:T(8,128)(2,1)} %param.8, bf16[256,1]{1,0:T(8,128)(2,1)S(1)} %stack.8, bf16[256,1]{1,0:T(8,128)(2,1)S(1)} %copy.29), dimensions={1} | concatenate | bytes 1574912 | tf_op jit(solution)/shard_map/concatenate | solution.py:102
  4.8 0.0 copy-start
  4.9 1.2 %all_to_all.16 = bf16[128,2,1538]{2,1,0:T(2,128)(2,1)} reshape(bf16[256,1538]{1,0:T(8,128)(2,1)S(1)} %concatenate.22) | data formatting | bytes 1574912 | tf_op jit(solution)/shard_map/all_to_all | solution.py:103
  6.1 17.8 %all-to-all-start = ((bf16[128,2,1538]{2,1,0:T(2,128)(2,1)}), bf16[128,2,1538]{2,1,0:T(2,128)(2,1)S(1)}, u32[]{:S(2)}, u32[]{:S(2)}) async-start(bf16[128,2,1538]{2,1,0:T(2,128)(2,1)} %all_to_all.16), calls=%async_computation | async-start | bytes 1703936 | tf_op jit(solution)/shard_map/all_to_all | solution.py:103
  23.9 0.0 copy-done
  23.9 0.1 compare_reduce_fusion
  24.0 0.1 fusion.19
  24.1 0.3 reduce-window.9
  24.4 0.1 slice.60
  24.5 0.1 slice_reduce_fusion
  24.6 0.1 bitcast_subtract_fusion
  24.7 26.4 %all-to-all-done = bf16[128,2,1538]{2,1,0:T(2,128)(2,1)S(1)} async-done(((bf16[128,2,1538]{2,1,0:T(2,128)(2,1)}), bf16[128,2,1538]{2,1,0:T(2,128)(2,1)S(1)}, u32[]{:S(2)}, u32[]{:S(2)}) %all-to-all-start) | async-done | bytes 787488 | tf_op jit(solution)/shard_map/all_to_all | solution.py:103
  51.1 0.6 all_to_all.18
  51.8 0.2 convert_reduce_fusion
  52.0 0.1 slice_convert_fusion
  52.1 0.1 select_reduce_fusion.1
  52.3 0.3 copy.32
  52.5 0.2 copy.31
  52.7 0.3 multiply_cosine_fusion
  53.0 0.1 subtract_convert_fusion
  53.1 0.1 multiply_subtract_fusion
  53.1 0.1 compare_and_fusion
  53.3 0.1 copy.30
  53.5 0.9 fusion.30
  54.4 0.3 convolution_convert_fusion.2
  54.7 0.2 copy.35
  54.9 0.2 copy.34
  55.1 0.1 reshape.281
  55.2 0.2 fusion.17
  55.4 0.1 broadcast_in_dim.92
  55.5 0.2 mul.143
  55.6 0.3 convolution_convert_fusion.1
  55.9 0.1 pad_maximum_fusion
  56.0 1.2 %all_to_all.19 = bf16[128,2,1536]{2,1,0:T(2,128)(2,1)} reshape(bf16[256,1536]{1,0:T(8,128)(2,1)S(1)} %pad_maximum_fusion) | data formatting | bytes 1572864 | tf_op jit(solution)/shard_map/all_to_all | solution.py:125
  57.1 6.2 %all-to-all-start.1 = ((bf16[128,2,1536]{2,1,0:T(2,128)(2,1)}), bf16[128,2,1536]{2,1,0:T(2,128)(2,1)S(1)}, u32[]{:S(2)}, u32[]{:S(2)}) async-start(bf16[128,2,1536]{2,1,0:T(2,128)(2,1)} %all_to_all.19), calls=%async_computation.1 | async-start | bytes 1572864 | tf_op jit(solution)/shard_map/all_to_all | solution.py:125
  63.3 0.1 broadcast_in_dim.93
  63.4 0.1 mul.146
  63.6 25.6 %all-to-all-done.1 = bf16[128,2,1536]{2,1,0:T(2,128)(2,1)S(1)} async-done(((bf16[128,2,1536]{2,1,0:T(2,128)(2,1)}), bf16[128,2,1536]{2,1,0:T(2,128)(2,1)S(1)}, u32[]{:S(2)}, u32[]{:S(2)}) %all-to-all-start.1) | async-done | bytes 786464 | tf_op jit(solution)/shard_map/all_to_all | solution.py:125
  89.2 0.3 all_to_all.21
  89.5 0.8 slice.81
  90.3 1.1 %convolution_convert_fusion = bf16[256,768]{1,0:T(8,128)(2,1)} fusion(bf16[256,1536]{1,0:T(8,128)(2,1)S(1)} %all_to_all.21, s32[256]{0:T(256)S(1)} %fusion.23), kind=kOutput, calls=%fused_computation.5 | convolution fusion | flops 100925440 | bytes 787456 | tf_op jit(solution)/shard_map/dot_general | solution.py:77
  (9 shorter events, 0.2 us)
Async XLA Ops:
  4.8 19.1 %copy-start = (s32[1,256]{1,0:T(1,128)S(1)}, s32[1,256]{1,0:T(1,128)}, u32[]{:S(2)}) copy-start(s32[1,256]{1,0:T(1,128)} %param.10) | copy-start | bytes 3076
  6.1 45.0 %all-to-all-start = ((bf16[128,2,1538]{2,1,0:T(2,128)(2,1)}), bf16[128,2,1538]{2,1,0:T(2,128)(2,1)S(1)}, u32[]{:S(2)}, u32[]{:S(2)}) async-start(bf16[128,2,1538]{2,1,0:T(2,128)(2,1)} %all_to_all.16), calls=%async_computation | async-start | bytes 1703936 | tf_op jit(solution)/shard_map/all_to_all | solution.py:103
  57.1 32.1 %all-to-all-start.1 = ((bf16[128,2,1536]{2,1,0:T(2,128)(2,1)}), bf16[128,2,1536]{2,1,0:T(2,128)(2,1)S(1)}, u32[]{:S(2)}, u32[]{:S(2)}) async-start(bf16[128,2,1536]{2,1,0:T(2,128)(2,1)} %all_to_all.19), calls=%async_computation.1 | async-start | bytes 1572864 | tf_op jit(solution)/shard_map/all_to_all | solution.py:125

commit v3 on v2

--- a/solution.py
+++ b/solution.py
@@ -66,8 +66,8 @@
 
 def one_hot_take(table, index):
     return jnp.sum(
-        jnp.where(index[:, None] == jnp.arange(table.shape[0], dtype=jnp.int32)[None, :], table[None, :], 0),
-        axis=1,
+        jnp.where(index[None, :] == jnp.arange(table.shape[0], dtype=jnp.int32)[:, None], table[:, None], 0),
+        axis=0,
     )
 
 
@@ -90,17 +90,16 @@
     devices = jnp.arange(device_count, dtype=jnp.int32)
     owner_row = page_owner[0]
     page_of_owner = jnp.sum(
-        jnp.where(owner_row[None, :] == devices[:, None], devices[None, :], 0), axis=1
+        jnp.where(owner_row[:, None] == devices[None, :], devices[:, None], 0), axis=0
     )
-    local_dealt = deal_index % row_count
-    page_meta = jnp.where(
-        arrival_rows % page_rows == 0,
-        jnp.repeat(owner_row, page_rows),
-        jnp.repeat(page_of_owner, page_rows),
+    local_dealt = (deal_index % row_count).reshape(device_count, page_rows)
+    page_meta = jnp.stack([owner_row, page_of_owner], axis=1)
+    meta = jnp.stack([local_dealt, page_meta], axis=2).astype(jnp.bfloat16)
+    outgoing = jnp.concatenate(
+        [part.reshape(device_count, page_rows, -1) for part in (queries, keys, values)] + [meta], axis=2
     )
-    meta = jnp.stack([local_dealt, page_meta], axis=1).astype(jnp.bfloat16)
-    outgoing = jnp.concatenate([queries, keys, values, meta], axis=1)
     received = lax.all_to_all(outgoing, "dev", split_axis=0, concat_axis=0, tiled=True)
+    received = received.reshape(row_count, -1)
 
     q_in = received[:, :query_width]
     k_in = received[:, query_width : query_width + key_width]

time: 91.6 us -> 95.8 us (1.046)
  local copies, waits for them, and re-layouts: 8.53 us -> 11.9 us
    reshape x2 -> x4, local copies, waits for them, and re-layouts: 0.31 us -> 3.8 us  [the longest x3 3.16 us: per_device(): part.reshape(device_count, page_rows, -1)]
    concatenate x1, local copies, waits for them, and re-layouts: 1.36 us -> 3.81 us  [per_device(): jnp.concatenate([part.reshape(device_count, page_rows, -1) for part in (q...]
    all_to_all x2 -> x0, local copies, waits for them, and re-layouts: 1.88 us -> none  [per_device(): lax.all_to_all(outgoing, 'dev', split_axis=0, concat_axis=0, tiled=True)]
where the time goes in v3:
time: 95.8 us; the launch traced here: 95.4 us
  waiting for transfers between devices  52 us (54%)
  starting transfers between devices  24 us (25%)
  local copies, waits for them, and re-layouts  11.9 us (12%)
  other arithmetic  4.12 us (4%)
  matrix products  2.52 us (3%)
    all_to_all x1, waiting for transfers between devices, per_device(): lax.all_to_all(outgoing, 'dev', split_axis=0, concat_axis=0, tiled=True)  26.4 us
    all_to_all x1, waiting for transfers between devices, per_device(): lax.all_to_all(going_back, 'dev', split_axis=0, concat_axis=0, tiled=True)  25.6 us
    all_to_all x1, starting transfers between devices, per_device(): lax.all_to_all(outgoing, 'dev', split_axis=0, concat_axis=0, tiled=True)  17.8 us
    all_to_all x1, starting transfers between devices, per_device(): lax.all_to_all(going_back, 'dev', split_axis=0, concat_axis=0, tiled=True)  6.18 us
    concatenate x1, local copies, waits for them, and re-layouts, per_device(): jnp.concatenate([part.reshape(device_count, page_rows, -1) for part in (q...  3.81 us
    reshape x3, local copies, waits for them, and re-layouts, per_device(): part.reshape(device_count, page_rows, -1)  3.16 us
  transfers between devices with their start and end apart: 2, of which 2 were waited for; matrix products, arithmetic and copies ran while one was open for 1% of the time, Pallas kernels for 0%

profile of v3, /device:TPU:6, one launch (start us, length us, event | category | flops | bytes accessed | tf_op | source)
XLA Modules:
  0.0 95.4 jit_solution(16318653195063486492)
XLA Ops:
  0.6 1.1 %reshape.240 = bf16[128,2,768]{2,1,0:T(2,128)(2,1)S(1)} reshape(bf16[256,768]{1,0:T(8,128)(2,1)} %param.6) | data formatting | bytes 786432 | tf_op jit(solution)/shard_map/reshape | solution.py:99
  1.8 1.0 %reshape.241 = bf16[128,2,384]{2,1,0:T(2,128)(2,1)S(1)} reshape(bf16[256,384]{1,0:T(8,128)(2,1)} %param.7) | data formatting | bytes 393216 | tf_op jit(solution)/shard_map/reshape | solution.py:99
  2.8 0.0 copy-start
  2.8 1.0 %reshape.242 = bf16[128,2,384]{2,1,0:T(2,128)(2,1)S(1)} reshape(bf16[256,384]{1,0:T(8,128)(2,1)} %param.8) | data formatting | bytes 393216 | tf_op jit(solution)/shard_map/reshape | solution.py:99
  3.8 0.7 convert_bitcast_fusion.1
  4.5 0.8 select_reduce_fusion.2
  5.2 0.1 copy.30
  5.4 0.7 fusion.21
  6.1 0.2 stack_reshape.5
  6.3 3.8 %concatenate.22 = bf16[128,2,1538]{2,1,0:T(2,128)(2,1)} concatenate(bf16[128,2,768]{2,1,0:T(2,128)(2,1)S(1)} %reshape.240, bf16[128,2,384]{2,1,0:T(2,128)(2,1)S(1)} %reshape.241, bf16[128,2,384]{2,1,0:T(2,128)(2,1)S(1)} %reshape.242, bf16[128,2,1]{2,1,0:T(2,128)(2,1)S(1)} %stack_reshape.5, bf16[128,2,1]{2,1,0:T(2,128)(2,1)S(1)} %copy.30), dimensions={2} | concatenate | bytes 1574912 | tf_op jit(solution)/shard_map/concatenate | solution.py:98
  10.1 17.8 %all-to-all-start = ((bf16[128,2,1538]{2,1,0:T(2,128)(2,1)}), bf16[128,2,1538]{2,1,0:T(2,128)(2,1)S(1)}, u32[]{:S(2)}, u32[]{:S(2)}) async-start(bf16[128,2,1538]{2,1,0:T(2,128)(2,1)} %concatenate.22), calls=%async_computation | async-start | bytes 1703936 | tf_op jit(solution)/shard_map/all_to_all | solution.py:101
  27.9 0.0 copy-done
  28.0 0.1 compare_reduce_fusion
  28.0 0.1 fusion.19
  28.1 0.3 reduce-window.9
  28.4 0.1 slice.60
  28.6 0.1 slice_reduce_fusion
  28.7 0.1 bitcast_subtract_fusion
  28.8 26.4 %all-to-all-done = bf16[128,2,1538]{2,1,0:T(2,128)(2,1)S(1)} async-done(((bf16[128,2,1538]{2,1,0:T(2,128)(2,1)}), bf16[128,2,1538]{2,1,0:T(2,128)(2,1)S(1)}, u32[]{:S(2)}, u32[]{:S(2)}) %all-to-all-start) | async-done | bytes 787488 | tf_op jit(solution)/shard_map/all_to_all | solution.py:101
  55.2 0.6 reshape.243
  55.8 0.2 convert_reduce_fusion
  56.0 0.1 slice_convert_fusion
  56.1 0.2 select_reduce_fusion.1
  56.4 0.3 copy.33
  56.7 0.2 copy.32
  56.8 0.3 multiply_cosine_fusion
  57.1 0.1 subtract_convert_fusion
  57.2 0.1 multiply_subtract_fusion
  57.3 0.1 compare_and_fusion
  57.4 0.1 copy.31
  57.6 0.9 fusion.29
  58.5 0.3 convolution_convert_fusion.2
  58.8 0.2 copy.36
  59.0 0.2 copy.35
  59.2 0.1 reshape.255
  59.3 0.2 fusion.17
  59.5 0.1 broadcast_in_dim.85
  59.6 0.2 mul.143
  59.7 0.3 convolution_convert_fusion.1
  60.0 0.1 pad_maximum_fusion
  60.1 1.2 %all_to_all.12 = bf16[128,2,1536]{2,1,0:T(2,128)(2,1)} reshape(bf16[256,1536]{1,0:T(8,128)(2,1)S(1)} %pad_maximum_fusion) | data formatting | bytes 1572864 | tf_op jit(solution)/shard_map/all_to_all | solution.py:124
  61.3 6.2 %all-to-all-start.1 = ((bf16[128,2,1536]{2,1,0:T(2,128)(2,1)}), bf16[128,2,1536]{2,1,0:T(2,128)(2,1)S(1)}, u32[]{:S(2)}, u32[]{:S(2)}) async-start(bf16[128,2,1536]{2,1,0:T(2,128)(2,1)} %all_to_all.12), calls=%async_computation.1 | async-start | bytes 1572864 | tf_op jit(solution)/shard_map/all_to_all | solution.py:124
  67.4 0.1 broadcast_in_dim.86
  67.5 0.1 mul.146
  67.7 25.6 %all-to-all-done.1 = bf16[128,2,1536]{2,1,0:T(2,128)(2,1)S(1)} async-done(((bf16[128,2,1536]{2,1,0:T(2,128)(2,1)}), bf16[128,2,1536]{2,1,0:T(2,128)(2,1)S(1)}, u32[]{:S(2)}, u32[]{:S(2)}) %all-to-all-start.1) | async-done | bytes 786464 | tf_op jit(solution)/shard_map/all_to_all | solution.py:124
  93.3 0.3 all_to_all.14
  93.6 0.8 slice.81
  94.4 1.1 %convolution_convert_fusion = bf16[256,768]{1,0:T(8,128)(2,1)} fusion(bf16[256,1536]{1,0:T(8,128)(2,1)S(1)} %all_to_all.14, s32[256]{0:T(256)S(1)} %fusion.22), kind=kOutput, calls=%fused_computation.5 | convolution fusion | flops 100925440 | bytes 787456 | tf_op jit(solution)/shard_map/dot_general | solution.py:77
  (10 shorter events, 0.2 us)
Async XLA Ops:
  2.8 25.2 %copy-start = (s32[1,256]{1,0:T(1,128)S(1)}, s32[1,256]{1,0:T(1,128)}, u32[]{:S(2)}) copy-start(s32[1,256]{1,0:T(1,128)} %param.10) | copy-start | bytes 3076
  10.1 45.0 %all-to-all-start = ((bf16[128,2,1538]{2,1,0:T(2,128)(2,1)}), bf16[128,2,1538]{2,1,0:T(2,128)(2,1)S(1)}, u32[]{:S(2)}, u32[]{:S(2)}) async-start(bf16[128,2,1538]{2,1,0:T(2,128)(2,1)} %concatenate.22), calls=%async_computation | async-start | bytes 1703936 | tf_op jit(solution)/shard_map/all_to_all | solution.py:101
  61.3 32.1 %all-to-all-start.1 = ((bf16[128,2,1536]{2,1,0:T(2,128)(2,1)}), bf16[128,2,1536]{2,1,0:T(2,128)(2,1)S(1)}, u32[]{:S(2)}, u32[]{:S(2)}) async-start(bf16[128,2,1536]{2,1,0:T(2,128)(2,1)} %all_to_all.12), calls=%async_computation.1 | async-start | bytes 1572864 | tf_op jit(solution)/shard_map/all_to_all | solution.py:124

commit v4 on v2

--- a/solution.py
+++ b/solution.py
@@ -3,6 +3,7 @@
 import jax
 import jax.numpy as jnp
 from jax import lax
+from jax.experimental import pallas as pl
 from jax.sharding import PartitionSpec as P
 
 QUERY_HEAD_COUNT = 8
@@ -56,6 +57,53 @@
     return out.reshape(rows, -1).astype(jnp.bfloat16)
 
 
+NT = (((1,), (1,)), ((), ()))
+
+
+def _pack_kernel(q_ref, k_ref, v_ref, d_ref, o_ref, out_ref):
+    rows = q_ref.shape[0]
+    pages = o_ref.shape[1]
+    page_rows = rows // pages
+    qw, kw = q_ref.shape[1], k_ref.shape[1]
+    owner = o_ref[...]
+    o_iota = lax.broadcasted_iota(jnp.int32, (pages, pages), 0)
+    p_iota = lax.broadcasted_iota(jnp.int32, (pages, pages), 1)
+    hits = (owner == o_iota).astype(jnp.bfloat16)
+    page_numbers = lax.broadcasted_iota(jnp.int32, (8, pages), 1).astype(jnp.bfloat16)
+    page_of_owner = lax.dot_general(page_numbers, hits, NT, preferred_element_type=jnp.float32)[0:1]
+    dealt = (d_ref[...] % rows).astype(jnp.float32)
+    width = rows + 2 * pages
+    src_row = lax.broadcasted_iota(jnp.int32, (128, width), 0)
+    src_col = lax.broadcasted_iota(jnp.int32, (128, width), 1)
+    dealt_ext = jnp.concatenate([dealt, jnp.zeros((1, 2 * pages), jnp.float32)], axis=1)
+    page_ext = jnp.concatenate(
+        [jnp.zeros((1, rows), jnp.float32), owner.astype(jnp.float32), page_of_owner], axis=1
+    )
+    sources = jnp.where(src_row == 0, dealt_ext, jnp.where(src_row == 1, page_ext, 0.0)).astype(jnp.bfloat16)
+    i = lax.broadcasted_iota(jnp.int32, (rows, width), 0)
+    m = lax.broadcasted_iota(jnp.int32, (rows, width), 1)
+    even = i % page_rows == 0
+    spread = (
+        (m == i)
+        | ((m - rows == i // page_rows) & even)
+        | ((m - rows - pages == i // page_rows) & ~even)
+    ).astype(jnp.bfloat16)
+    meta = lax.dot_general(spread, sources, NT, preferred_element_type=jnp.float32)
+    out_ref[:, 0:qw] = q_ref[...]
+    out_ref[:, qw : qw + kw] = k_ref[...]
+    out_ref[:, qw + kw : qw + 2 * kw] = v_ref[...]
+    out_ref[:, qw + 2 * kw :] = meta.astype(jnp.bfloat16)
+
+
+def pack_outgoing(queries, keys, values, deal_index, page_owner):
+    rows = queries.shape[0]
+    width = queries.shape[1] + 2 * keys.shape[1] + 128
+    return pl.pallas_call(
+        _pack_kernel,
+        out_shape=jax.ShapeDtypeStruct((rows, width), queries.dtype),
+    )(queries, keys, values, deal_index.reshape(1, rows), page_owner)
+
+
 def row_permute(matrix, target_rows):
     rows = matrix.shape[0]
     onehot = (jnp.arange(rows, dtype=jnp.int32)[:, None] == target_rows[None, :]).astype(
@@ -87,19 +135,7 @@
     dealt_positions = positions_of(request_labels)
 
     arrival_rows = jnp.arange(row_count, dtype=jnp.int32)
-    devices = jnp.arange(device_count, dtype=jnp.int32)
-    owner_row = page_owner[0]
-    page_of_owner = jnp.sum(
-        jnp.where(owner_row[None, :] == devices[:, None], devices[None, :], 0), axis=1
-    )
-    local_dealt = deal_index % row_count
-    page_meta = jnp.where(
-        arrival_rows % page_rows == 0,
-        jnp.repeat(owner_row, page_rows),
-        jnp.repeat(page_of_owner, page_rows),
-    )
-    meta = jnp.stack([local_dealt, page_meta], axis=1).astype(jnp.bfloat16)
-    outgoing = jnp.concatenate([queries, keys, values, meta], axis=1)
+    outgoing = pack_outgoing(queries, keys, values, deal_index, page_owner)
     received = lax.all_to_all(outgoing, "dev", split_axis=0, concat_axis=0, tiled=True)
 
     q_in = received[:, :query_width]

time: 91.6 us -> 91.2 us (level)
  Pallas kernels: 0 us -> 2.42 us
  other arithmetic: 3.39 us -> 1.93 us
  local copies, waits for them, and re-layouts: 8.53 us -> 7.22 us
    pallas_call x0 -> x1, Pallas kernels: none -> 2.42 us  [pack_outgoing(): pl.pallas_call(_pack_kernel, out_shape=jax.ShapeDtypeStruct((rows, width)...]
    all_to_all x2, local copies, waits for them, and re-layouts: 1.88 us -> 3.29 us  [per_device(): lax.all_to_all(outgoing, 'dev', split_axis=0, concat_axis=0, tiled=True)]
    concatenate x1 -> x0, local copies, waits for them, and re-layouts: 1.36 us -> none  [per_device(): outgoing = jnp.concatenate([queries, keys, values, meta], axis=1)]
where the time goes in v4:
time: 91.2 us; the launch traced here: 90.9 us
  waiting for transfers between devices  52 us (57%)
  starting transfers between devices  24 us (26%)
  local copies, waits for them, and re-layouts  7.22 us (8%)
  matrix products  2.53 us (3%)
  Pallas kernels  2.42 us (3%)
  other arithmetic  1.93 us (2%)
    all_to_all x1, waiting for transfers between devices, per_device(): lax.all_to_all(outgoing, 'dev', split_axis=0, concat_axis=0, tiled=True)  26.4 us
    all_to_all x1, waiting for transfers between devices, per_device(): lax.all_to_all(going_back, 'dev', split_axis=0, concat_axis=0, tiled=True)  25.6 us
    all_to_all x1, starting transfers between devices, per_device(): lax.all_to_all(outgoing, 'dev', split_axis=0, concat_axis=0, tiled=True)  17.8 us
    all_to_all x1, starting transfers between devices, per_device(): lax.all_to_all(going_back, 'dev', split_axis=0, concat_axis=0, tiled=True)  6.18 us
    all_to_all x2, local copies, waits for them, and re-layouts, per_device(): lax.all_to_all(outgoing, 'dev', split_axis=0, concat_axis=0, tiled=True)  3.29 us
    pallas_call x1, Pallas kernels, pack_outgoing(): pl.pallas_call(_pack_kernel, out_shape=jax.ShapeDtypeStruct((rows, width)...  2.42 us
  transfers between devices with their start and end apart: 2, of which 2 were waited for; matrix products, arithmetic and copies ran while one was open for 1% of the time, Pallas kernels for 0%

profile of v4, /device:TPU:6, one launch (start us, length us, event | category | flops | bytes accessed | tf_op | source)
XLA Modules:
  0.0 90.9 jit_solution(18444246102407182315)
XLA Ops:
  0.6 2.4 %shard_map.77 = bf16[256,1664]{1,0:T(8,128)(2,1)} custom-call(bf16[256,768]{1,0:T(8,128)(2,1)} %q_ref.1, bf16[256,384]{1,0:T(8,128)(2,1)} %k_ref.1, bf16[256,384]{1,0:T(8,128)(2,1)} %v_ref.1, s32[1,256]{1,0:T(1,128)} %bitcast.49, s32[1,128]{1,0:T(1,128)} %o_ref.1), custom_call_target="tpu_custom_call" | custom-call | tf_op jit(solution)/shard_map/pallas_call | solution.py:101
  3.1 0.0 copy-start
  3.1 3.0 %all_to_all.16 = bf16[128,2,1664]{2,1,0:T(2,128)(2,1)} reshape(bf16[256,1664]{1,0:T(8,128)(2,1)} %shard_map.77) | data formatting | bytes 1703936 | tf_op jit(solution)/shard_map/all_to_all | solution.py:139
  6.0 17.8 %all-to-all-start = ((bf16[128,2,1664]{2,1,0:T(2,128)(2,1)}), bf16[128,2,1664]{2,1,0:T(2,128)(2,1)S(1)}, u32[]{:S(2)}, u32[]{:S(2)}) async-start(bf16[128,2,1664]{2,1,0:T(2,128)(2,1)} %all_to_all.16), calls=%async_computation | async-start | bytes 1703936 | tf_op jit(solution)/shard_map/all_to_all | solution.py:139
  23.8 0.0 copy-done
  23.9 0.1 compare_reduce_fusion
  23.9 0.1 fusion.19
  24.0 0.3 reduce-window.9
  24.3 0.1 slice.60
  24.5 0.1 slice_reduce_fusion
  24.6 0.1 bitcast_subtract_fusion
  24.6 26.4 %all-to-all-done = bf16[128,2,1664]{2,1,0:T(2,128)(2,1)S(1)} async-done(((bf16[128,2,1664]{2,1,0:T(2,128)(2,1)}), bf16[128,2,1664]{2,1,0:T(2,128)(2,1)S(1)}, u32[]{:S(2)}, u32[]{:S(2)}) %all-to-all-start) | async-done | bytes 852000 | tf_op jit(solution)/shard_map/all_to_all | solution.py:139
  51.1 0.3 all_to_all.18
  51.4 0.2 convert_reduce_fusion
  51.6 0.1 slice_convert_fusion
  51.7 0.1 select_reduce_fusion.1
  51.9 0.3 copy.25
  52.1 0.2 copy.24
  52.3 0.3 multiply_cosine_fusion
  52.6 0.1 subtract_convert_fusion
  52.7 0.1 multiply_subtract_fusion
  52.8 0.1 compare_and_fusion
  52.9 0.1 copy.23
  53.1 0.9 fusion.27
  54.0 0.3 convolution_convert_fusion.2
  54.3 0.2 copy.28
  54.5 0.2 copy.27
  54.7 0.1 reshape.242
  54.8 0.2 fusion.17
  55.0 0.1 broadcast_in_dim.74
  55.1 0.2 mul.143
  55.2 0.3 convolution_convert_fusion.1
  55.5 0.1 pad_maximum_fusion
  55.6 1.2 %all_to_all.19 = bf16[128,2,1536]{2,1,0:T(2,128)(2,1)} reshape(bf16[256,1536]{1,0:T(8,128)(2,1)S(1)} %pad_maximum_fusion) | data formatting | bytes 1572864 | tf_op jit(solution)/shard_map/all_to_all | solution.py:161
  56.7 6.2 %all-to-all-start.1 = ((bf16[128,2,1536]{2,1,0:T(2,128)(2,1)}), bf16[128,2,1536]{2,1,0:T(2,128)(2,1)S(1)}, u32[]{:S(2)}, u32[]{:S(2)}) async-start(bf16[128,2,1536]{2,1,0:T(2,128)(2,1)} %all_to_all.19), calls=%async_computation.1 | async-start | bytes 1572864 | tf_op jit(solution)/shard_map/all_to_all | solution.py:161
  62.9 0.1 broadcast_in_dim.76
  63.0 0.1 mul.146
  63.2 25.6 %all-to-all-done.1 = bf16[128,2,1536]{2,1,0:T(2,128)(2,1)S(1)} async-done(((bf16[128,2,1536]{2,1,0:T(2,128)(2,1)}), bf16[128,2,1536]{2,1,0:T(2,128)(2,1)S(1)}, u32[]{:S(2)}, u32[]{:S(2)}) %all-to-all-start.1) | async-done | bytes 786464 | tf_op jit(solution)/shard_map/all_to_all | solution.py:161
  88.8 0.3 all_to_all.21
  89.1 0.8 slice.81
  89.9 1.1 %convolution_convert_fusion = bf16[256,768]{1,0:T(8,128)(2,1)} fusion(bf16[256,1536]{1,0:T(8,128)(2,1)S(1)} %all_to_all.21, s32[256]{0:T(256)S(1)} %fusion.20), kind=kOutput, calls=%fused_computation.5 | convolution fusion | flops 100925440 | bytes 787456 | tf_op jit(solution)/shard_map/dot_general | solution.py:125
  (8 shorter events, 0.2 us)
Async XLA Ops:
  3.1 20.8 %copy-start = (s32[1,256]{1,0:T(1,128)S(1)}, s32[1,256]{1,0:T(1,128)}, u32[]{:S(2)}) copy-start(s32[1,256]{1,0:T(1,128)} %param.10) | copy-start | bytes 3076
  6.0 45.0 %all-to-all-start = ((bf16[128,2,1664]{2,1,0:T(2,128)(2,1)}), bf16[128,2,1664]{2,1,0:T(2,128)(2,1)S(1)}, u32[]{:S(2)}, u32[]{:S(2)}) async-start(bf16[128,2,1664]{2,1,0:T(2,128)(2,1)} %all_to_all.16), calls=%async_computation | async-start | bytes 1703936 | tf_op jit(solution)/shard_map/all_to_all | solution.py:139
  56.7 32.1 %all-to-all-start.1 = ((bf16[128,2,1536]{2,1,0:T(2,128)(2,1)}), bf16[128,2,1536]{2,1,0:T(2,128)(2,1)S(1)}, u32[]{:S(2)}, u32[]{:S(2)}) async-start(bf16[128,2,1536]{2,1,0:T(2,128)(2,1)} %all_to_all.19), calls=%async_computation.1 | async-start | bytes 1572864 | tf_op jit(solution)/shard_map/all_to_all | solution.py:161

commit v5 on v4

--- a/solution.py
+++ b/solution.py
@@ -60,11 +60,10 @@
 NT = (((1,), (1,)), ((), ()))
 
 
-def _pack_kernel(q_ref, k_ref, v_ref, d_ref, o_ref, out_ref):
-    rows = q_ref.shape[0]
+def _pack_kernel(d_ref, o_ref, out_ref):
+    rows = d_ref.shape[1]
     pages = o_ref.shape[1]
     page_rows = rows // pages
-    qw, kw = q_ref.shape[1], k_ref.shape[1]
     owner = o_ref[...]
     o_iota = lax.broadcasted_iota(jnp.int32, (pages, pages), 0)
     p_iota = lax.broadcasted_iota(jnp.int32, (pages, pages), 1)
@@ -89,19 +88,16 @@
         | ((m - rows - pages == i // page_rows) & ~even)
     ).astype(jnp.bfloat16)
     meta = lax.dot_general(spread, sources, NT, preferred_element_type=jnp.float32)
-    out_ref[:, 0:qw] = q_ref[...]
-    out_ref[:, qw : qw + kw] = k_ref[...]
-    out_ref[:, qw + kw : qw + 2 * kw] = v_ref[...]
-    out_ref[:, qw + 2 * kw :] = meta.astype(jnp.bfloat16)
+    out_ref[...] = meta.astype(jnp.bfloat16)
 
 
 def pack_outgoing(queries, keys, values, deal_index, page_owner):
     rows = queries.shape[0]
-    width = queries.shape[1] + 2 * keys.shape[1] + 128
-    return pl.pallas_call(
+    meta = pl.pallas_call(
         _pack_kernel,
-        out_shape=jax.ShapeDtypeStruct((rows, width), queries.dtype),
-    )(queries, keys, values, deal_index.reshape(1, rows), page_owner)
+        out_shape=jax.ShapeDtypeStruct((rows, 128), queries.dtype),
+    )(deal_index.reshape(1, rows), page_owner)
+    return jnp.concatenate([queries, keys, values, meta], axis=1)
 
 
 def row_permute(matrix, target_rows):

time: 91.2 us -> 90 us (0.987)
  local copies, waits for them, and re-layouts: 7.22 us -> 5.48 us
  other arithmetic: 1.93 us -> 3.22 us
    all_to_all x2, local copies, waits for them, and re-layouts: 3.29 us -> 1.55 us  [per_device(): lax.all_to_all(outgoing, 'dev', split_axis=0, concat_axis=0, tiled=True)]
    concatenate x0 -> x1, other arithmetic: none -> 1.29 us  [pack_outgoing(): return jnp.concatenate([queries, keys, values, meta], axis=1)]
where the time goes in v5:
time: 90 us; the launch traced here: 89.7 us
  waiting for transfers between devices  52 us (58%)
  starting transfers between devices  24 us (27%)
  local copies, waits for them, and re-layouts  5.48 us (6%)
  other arithmetic  3.22 us (4%)
  matrix products  2.53 us (3%)
  Pallas kernels  1.65 us (2%)
    all_to_all x1, waiting for transfers between devices, per_device(): lax.all_to_all(outgoing, 'dev', split_axis=0, concat_axis=0, tiled=True)  26.4 us
    all_to_all x1, waiting for transfers between devices, per_device(): lax.all_to_all(going_back, 'dev', split_axis=0, concat_axis=0, tiled=True)  25.6 us
    all_to_all x1, starting transfers between devices, per_device(): lax.all_to_all(outgoing, 'dev', split_axis=0, concat_axis=0, tiled=True)  17.8 us
    all_to_all x1, starting transfers between devices, per_device(): lax.all_to_all(going_back, 'dev', split_axis=0, concat_axis=0, tiled=True)  6.18 us
  transfers between devices with their start and end apart: 2, of which 2 were waited for; matrix products, arithmetic and copies ran while one was open for 1% of the time, Pallas kernels for 0%

profile of v5, /device:TPU:6, one launch (start us, length us, event | category | flops | bytes accessed | tf_op | source)
XLA Modules:
  0.0 89.7 jit_solution(8807674505643277991)
XLA Ops:
  0.6 1.7 %shard_map.77 = bf16[256,128]{1,0:T(8,128)(2,1)} custom-call(s32[1,256]{1,0:T(1,128)} %bitcast.49, s32[1,128]{1,0:T(1,128)} %o_ref.1), custom_call_target="tpu_custom_call" | custom-call | tf_op jit(solution)/shard_map/pallas_call | solution.py:96
  2.3 1.3 %pad_maximum_fusion = bf16[256,1664]{1,0:T(8,128)(2,1)S(1)} fusion(bf16[256,128]{1,0:T(8,128)(2,1)} %shard_map.77, bf16[256,384]{1,0:T(8,128)(2,1)} %param.8, bf16[256,384]{1,0:T(8,128)(2,1)} %param.7, bf16[256,768]{1,0:T(8,128)(2,1)} %param.6), kind=kLoop, calls=%fused_computation.11 | loop fusion | flops 3407872 | bytes 1703936 | tf_op jit(solution)/shard_map/concatenate | solution.py:100
  3.6 0.0 copy-start
  3.6 1.2 %all_to_all.16 = bf16[128,2,1664]{2,1,0:T(2,128)(2,1)} reshape(bf16[256,1664]{1,0:T(8,128)(2,1)S(1)} %pad_maximum_fusion) | data formatting | bytes 1703936 | tf_op jit(solution)/shard_map/all_to_all | solution.py:135
  4.8 17.8 %all-to-all-start = ((bf16[128,2,1664]{2,1,0:T(2,128)(2,1)}), bf16[128,2,1664]{2,1,0:T(2,128)(2,1)S(1)}, u32[]{:S(2)}, u32[]{:S(2)}) async-start(bf16[128,2,1664]{2,1,0:T(2,128)(2,1)} %all_to_all.16), calls=%async_computation | async-start | bytes 1703936 | tf_op jit(solution)/shard_map/all_to_all | solution.py:135
  22.6 0.0 copy-done
  22.6 0.1 compare_reduce_fusion
  22.7 0.1 fusion.19
  22.8 0.3 reduce-window.9
  23.1 0.1 slice.60
  23.3 0.1 slice_reduce_fusion
  23.4 0.1 bitcast_subtract_fusion
  23.4 26.4 %all-to-all-done = bf16[128,2,1664]{2,1,0:T(2,128)(2,1)S(1)} async-done(((bf16[128,2,1664]{2,1,0:T(2,128)(2,1)}), bf16[128,2,1664]{2,1,0:T(2,128)(2,1)S(1)}, u32[]{:S(2)}, u32[]{:S(2)}) %all-to-all-start) | async-done | bytes 852000 | tf_op jit(solution)/shard_map/all_to_all | solution.py:135
  49.8 0.3 all_to_all.18
  50.2 0.2 convert_reduce_fusion
  50.4 0.1 slice_convert_fusion
  50.5 0.1 select_reduce_fusion.1
  50.7 0.3 copy.20
  50.9 0.2 copy.19
  51.1 0.3 multiply_cosine_fusion
  51.4 0.1 subtract_convert_fusion
  51.5 0.1 multiply_subtract_fusion
  51.5 0.1 compare_and_fusion
  51.7 0.1 copy.18
  51.9 0.9 fusion.27
  52.8 0.3 convolution_convert_fusion.2
  53.1 0.2 copy.23
  53.3 0.2 copy.22
  53.5 0.1 reshape.242
  53.6 0.2 fusion.17
  53.8 0.1 broadcast_in_dim.74
  53.9 0.2 mul.143
  54.0 0.3 convolution_convert_fusion.1
  54.3 0.1 pad_maximum_fusion.1
  54.4 1.2 %all_to_all.19 = bf16[128,2,1536]{2,1,0:T(2,128)(2,1)} reshape(bf16[256,1536]{1,0:T(8,128)(2,1)S(1)} %pad_maximum_fusion.1) | data formatting | bytes 1572864 | tf_op jit(solution)/shard_map/all_to_all | solution.py:157
  55.5 6.2 %all-to-all-start.1 = ((bf16[128,2,1536]{2,1,0:T(2,128)(2,1)}), bf16[128,2,1536]{2,1,0:T(2,128)(2,1)S(1)}, u32[]{:S(2)}, u32[]{:S(2)}) async-start(bf16[128,2,1536]{2,1,0:T(2,128)(2,1)} %all_to_all.19), calls=%async_computation.1 | async-start | bytes 1572864 | tf_op jit(solution)/shard_map/all_to_all | solution.py:157
  61.7 0.1 broadcast_in_dim.76
  61.8 0.1 mul.146
  62.0 25.6 %all-to-all-done.1 = bf16[128,2,1536]{2,1,0:T(2,128)(2,1)S(1)} async-done(((bf16[128,2,1536]{2,1,0:T(2,128)(2,1)}), bf16[128,2,1536]{2,1,0:T(2,128)(2,1)S(1)}, u32[]{:S(2)}, u32[]{:S(2)}) %all-to-all-start.1) | async-done | bytes 786464 | tf_op jit(solution)/shard_map/all_to_all | solution.py:157
  87.6 0.3 all_to_all.21
  87.9 0.8 slice.81
  88.7 1.1 %convolution_convert_fusion = bf16[256,768]{1,0:T(8,128)(2,1)} fusion(bf16[256,1536]{1,0:T(8,128)(2,1)S(1)} %all_to_all.21, s32[256]{0:T(256)S(1)} %fusion.20), kind=kOutput, calls=%fused_computation.5 | convolution fusion | flops 100925440 | bytes 787456 | tf_op jit(solution)/shard_map/dot_general | solution.py:121
  (8 shorter events, 0.2 us)
Async XLA Ops:
  3.6 19.1 %copy-start = (s32[1,256]{1,0:T(1,128)S(1)}, s32[1,256]{1,0:T(1,128)}, u32[]{:S(2)}) copy-start(s32[1,256]{1,0:T(1,128)} %param.10) | copy-start | bytes 3076
  4.8 45.0 %all-to-all-start = ((bf16[128,2,1664]{2,1,0:T(2,128)(2,1)}), bf16[128,2,1664]{2,1,0:T(2,128)(2,1)S(1)}, u32[]{:S(2)}, u32[]{:S(2)}) async-start(bf16[128,2,1664]{2,1,0:T(2,128)(2,1)} %all_to_all.16), calls=%async_computation | async-start | bytes 1703936 | tf_op jit(solution)/shard_map/all_to_all | solution.py:135
  55.5 32.1 %all-to-all-start.1 = ((bf16[128,2,1536]{2,1,0:T(2,128)(2,1)}), bf16[128,2,1536]{2,1,0:T(2,128)(2,1)S(1)}, u32[]{:S(2)}, u32[]{:S(2)}) async-start(bf16[128,2,1536]{2,1,0:T(2,128)(2,1)} %all_to_all.19), calls=%async_computation.1 | async-start | bytes 1572864 | tf_op jit(solution)/shard_map/all_to_all | solution.py:157
